TPU v7x, 256 devices: a whole 4x4x8 slice. The times are simulated.
256 devices in a mesh: snap: 4 (over x), line: 64 (over z, y, core).
Axes of the slice: x: 4, y: 4, z: 8, core: 2. Of those that a mesh axis runs over, the one named last changes fastest.
Arguments:
- ptdf_rows: float32 [8192, 20480], P('line'), may hold values from -4 to 4
- plan: float32 [5120, 2048], P(('snap', 'line')), may hold values from 0 to 0.15
- unit_bus: int32 [5120], replicated, may hold values from 0 to 20479
- min_up: int32 [5120], P(('snap', 'line')), may hold values from 1 to 24, as said below
- ramp_lag: int32 [5120], P(('snap', 'line')), may hold values from 1 to 6, as said below
- load_share: float32 [20480], replicated, may hold values from 0.004 to 0.04
- system_load: float32 [2048], P('snap'), may hold values from 0.6 to 1.4
- corridor_order: int32 [4], replicated, may hold values from 0 to 3, each once
- corridor_buses: int32 [4, 2], replicated, may hold values from 0 to 20479, as said below
- corridor_owner: int32 [4], replicated, may hold values from 0 to 63
- corridor_row: int32 [4], replicated, may hold values from 0 to 127
- corridor_ratio: float32 [4], replicated, may hold values from 0.5 to 2
Outputs:
- flows: float32 [8192, 2048], P('line', 'snap')
- corridor_sens: float32 [4, 20480], replicated
Inputs may be any that keep to these rules, and one draw needn't show every extreme that they name: `min_up`: some unit has a window of exactly 24. `ramp_lag`: some unit has a lag of exactly 6. `corridor_buses`: the two buses of a corridor differ.
All inputs are finite; a program needn't handle non-finite values.
Results may differ from a plain program's by a relative error of at most 0.000098.
Values sent between devices are 32-bit elements; how exact they have to be, the bound alone decides.
No kernel may reach another device: no remote copies, remote signals or barrier semaphores. Data moves between devices by JAX's collectives and lax.ppermute only.
A program may use at most 128 MiB of HBM per device.

v0:
```python
import jax
import jax.numpy as jnp
from jax import lax
from jax.sharding import Mesh
from jax.sharding import PartitionSpec as P

WMAX = 24
NC = 4
LINE = ("line_0", "line_1", "line_2")
SNAP_LINE = ("snap", "line_0", "line_1", "line_2")
ramp_gain = 0.5


def in_blocks(x, dim, peers):
    before, after = (x.shape[:dim], x.shape[dim + 1 :])
    return jnp.moveaxis(x.reshape(*before, peers, -1, *after), dim, 0)


def sum_at_owner(x, axis, dim):
    tiles = in_blocks(x, dim, lax.axis_size(axis))
    arrived = lax.all_to_all(tiles, axis, split_axis=0, concat_axis=0, tiled=True)
    return arrived.sum(axis=0)


def summed_rows(x, axes, dim):
    far, near = axes
    tiles = in_blocks(x, dim, lax.axis_size(far))
    nearer = sum_at_owner(tiles, near, dim + 1)
    arrived = lax.all_to_all(nearer, far, split_axis=0, concat_axis=0, tiled=True)
    return arrived.sum(axis=0)


def padded_to(lines, peers):
    spare = -len(lines) % peers
    return jnp.pad(lines, [(0, spare)] + [(0, 0)] * (lines.ndim - 1))


def copy_for_each(x, axis):
    peers = lax.axis_size(axis)
    return lax.all_to_all(jnp.broadcast_to(x[None], (peers, *x.shape)), axis, 0, 0, tiled=True)


def joined_along(tiles, dim):
    lengths = list(tiles.shape[1:])
    lengths[dim] *= tiles.shape[0]
    return jnp.moveaxis(tiles, 0, dim).reshape(lengths)


def gathered_by_axis(x, axes, dim):
    far, near = axes
    leading = copy_for_each(x, far)
    tiles = jnp.swapaxes(copy_for_each(leading, near), 0, 1)
    return joined_along(tiles.reshape(-1, *x.shape), dim)


def total_of(x, axes):
    own = summed_rows(padded_to(x, lax.axis_size(axes[0]) * lax.axis_size(axes[1])), axes, 0)
    whole = gathered_by_axis(own, axes, 0)
    return whole[: len(x)].reshape(x.shape)


def together(arrays, axis):
    ends = [0]
    for a in arrays:
        ends.append(ends[-1] + a.size)
    subtotal = total_of(jnp.concatenate([a.ravel() for a in arrays]), axis)
    return tuple((subtotal[b:e].reshape(a.shape) for a, b, e in zip(arrays, ends, ends[1:])))


def body(
    ptdf_rows,
    plan,
    unit_bus,
    min_up,
    ramp_lag,
    load_share,
    system_load,
    corridor_order,
    corridor_buses,
    corridor_owner,
    corridor_row,
    corridor_ratio,
):
    unit_count, horizon = plan.shape
    snap_count = lax.axis_size("snap")
    line_count = lax.axis_size(LINE)
    padded = jnp.pad(plan, ((0, 0), (WMAX, 0)))
    inverse = 1.0 / min_up.astype(jnp.float32)
    held_mean = jnp.zeros(plan.shape, jnp.float32)
    lagged = jnp.zeros(plan.shape, jnp.float32)
    for offset in range(WMAX):
        shifted = padded[:, WMAX - offset : WMAX - offset + horizon]
        held_mean = held_mean + shifted * jnp.where(offset < min_up, inverse, 0.0)[:, None]
        lagged = lagged + shifted * (ramp_lag == offset).astype(jnp.float32)[:, None]
    dispatch = held_mean + ramp_gain * (plan - lagged)
    unit_blocks = lax.all_to_all(dispatch, "snap", split_axis=1, concat_axis=0, tiled=True)
    order_ids = unit_bus.reshape(snap_count, line_count, unit_count).transpose(1, 0, 2).reshape(-1)
    columns = jnp.take(ptdf_rows, order_ids, axis=1)
    gen_flows = jnp.dot(
        columns,
        lax.all_gather(unit_blocks, LINE, axis=0, tiled=True),
        preferred_element_type=jnp.float32,
        precision=lax.Precision.HIGHEST,
    )
    load_flows = jnp.dot(
        ptdf_rows, load_share, preferred_element_type=jnp.float32, precision=lax.Precision.HIGHEST
    )
    base = gen_flows - load_flows[:, None] * system_load[None, :]
    here = lax.axis_index(LINE)
    picked_rows = []
    picked_flows = []
    for step in range(NC):
        chosen = corridor_order[step]
        local_row = corridor_row[chosen]
        mine = corridor_owner[chosen] == here
        picked_rows.append(jnp.where(mine, ptdf_rows[local_row], 0.0))
        picked_flows.append(jnp.where(mine, base[local_row], 0.0))
    all_rows, all_flows = together(
        (jnp.stack(picked_rows), jnp.stack(picked_flows)), (("line_0", "line_1"), "line_2")
    )
    coeff_list = []
    sens_list = []
    shift_list = []
    ends_list = []
    for step in range(NC):
        chosen = corridor_order[step]
        bus_from = corridor_buses[chosen, 0]
        bus_to = corridor_buses[chosen, 1]
        ratio = corridor_ratio[chosen]
        coefficient = ptdf_rows[:, bus_from] - ptdf_rows[:, bus_to]
        for prior in range(step):
            coefficient = coefficient - coeff_list[prior] * (
                sens_list[prior][bus_from] - sens_list[prior][bus_to]
            )
        initial = all_rows[step]
        current = initial
        line_flow = all_flows[step]
        row_coeffs = []
        for prior in range(step):
            prior_from, prior_to = ends_list[prior]
            value = initial[prior_from] - initial[prior_to]
            for earlier in range(prior):
                value = value - row_coeffs[earlier] * (
                    sens_list[earlier][prior_from] - sens_list[earlier][prior_to]
                )
            row_coeffs.append(value)
        for prior in range(step):
            current = current - row_coeffs[prior] * sens_list[prior]
            line_flow = line_flow - row_coeffs[prior] * shift_list[prior]
        weight = ratio / (1.0 + ratio * jnp.abs(current[bus_from] - current[bus_to]))
        coeff_list.append(coefficient)
        sens_list.append(weight * current)
        shift_list.append(weight * line_flow)
        ends_list.append((bus_from, bus_to))
    flows = base
    for step in range(NC):
        flows = flows - coeff_list[step][:, None] * shift_list[step][None, :]
    return (flows, jnp.stack(sens_list))


def solution(mesh):
    torus = Mesh(
        mesh.devices.reshape(mesh.shape["snap"], 8, 4, 2), ("snap", "line_0", "line_1", "line_2")
    )
    in_specs = (
        P(LINE, None),
        P(SNAP_LINE, None),
        P(),
        P(SNAP_LINE),
        P(SNAP_LINE),
        P(),
        P("snap"),
        P(),
        P(),
        P(),
        P(),
        P(),
    )
    out_specs = (P(LINE, "snap"), P())
    return jax.shard_map(body, mesh=torus, in_specs=in_specs, out_specs=out_specs, check_vma=False)
```

profile of v0, /device:TPU:1, one launch (start us, length us, event | category | flops | bytes accessed | tf_op | source)
XLA Modules:
  0.0 217.8 jit_solution(7106054973172409046)
XLA Ops:
  7.2 0.0 copy-start
  7.2 0.0 all-gather.2.cloned.1.call-start
  7.2 0.7 compare_select_fusion.25
  8.0 0.7 compare_select_fusion.24
  8.6 0.7 compare_convert_fusion.23
  9.3 6.7 %multiply_add_fusion = f32[20,2048]{1,0:T(8,128)S(1)} fusion(f32[20,2048]{1,0:T(8,128)} %param.13, f32[20]{0:T(128)S(1)} %get-tuple-element.133, f32[20]{0:T(128)S(1)} %get-tuple-element.134, f32[20]{0:T(128)S(1)} %get-tuple-element.112, f32[20]{0:T(128)S(1)} %get-tuple-element.113, f32[20]{0:T(128)S(1)} %get-tuple-element.114, ...), kind=kLoop, calls=%fused_computation.11 | loop fusion | flops 3973120 | bytes 331520 | tf_op jit(solution)/shard_map/add | solution.py:95
  16.0 0.1 all_to_all.30
  16.1 0.1 copy.27
  16.2 9.8 %all_to_all.44 = f32[20,4,512]{2,0,1:T(8,128)S(1)} all-to-all(f32[20,4,512]{2,0,1:T(8,128)S(1)} %copy.27), channel_id=1, replica_groups=mesh['snap'=4,'line_0'=8,'line_1'=4,'line_2'=2] {'snap'}, dimensions={1} | all-to-all | bytes 327680 | tf_op jit(solution)/shard_map/all_to_all | solution.py:96
  26.0 0.7 all_to_all.33
  26.7 0.0 all-gather.2.cloned.1.call-update
  26.7 0.9 reshape.185
  27.6 0.1 copy.24
  27.7 0.2 reshape.187
  27.9 0.2 reshape.186
  28.0 1.4 fusion.31
  36.8 1.5 fusion.29
  43.4 11.8 %copy.26 = f32[128,20480]{0,1:T(8,128)} copy(f32[128,20480]{1,0:T(8,128)} %param.12) | data formatting | bytes 20971520 | tf_op args[0]
  60.3 2.0 broadcast_select_fusion.3
  62.3 0.3 maximum_bitcast_fusion
  62.7 17.4 %gather_fusion = f32[5120,128]{1,0:T(8,128)S(1)} fusion(f32[128,20480]{0,1:T(8,128)} %copy.26, s32[5120]{0:T(1024)S(1)} %broadcast_clamp_fusion), kind=kCustom, calls=%fused_computation | custom fusion | bytes 5263360 | tf_op jit(solution)/shard_map/jit(_take)/gather | solution.py:98
  80.1 0.0 copy-start.3
  80.1 0.0 copy-done
  80.1 10.9 %convolution_bitcast_fusion = f32[128]{0:T(128)S(1)} fusion(f32[128,20480]{1,0:T(8,128)} %param.12, f32[20480,1]{0,1:T(1,128)S(1)} %bitcast.64), kind=kOutput, calls=%fused_computation.6 | convolution fusion | flops 31457280 | bytes 10568192 | tf_op jit(solution)/shard_map/dot_general | solution.py:105
  91.0 0.0 copy-start.1
  91.0 0.0 copy-start.2
  91.0 24.8 %all-gather.2.cloned.1.call-done = f32[5120,512]{1,0:T(8,128)} async-done(((f32[80,512]{1,0:T(8,128)}), f32[5120,512]{1,0:T(8,128)}) %all-gather.2.cloned.1.call-update) | async-done | bytes 10485776 | tf_op jit(solution)/shard_map/all_gather | solution.py:101
  115.9 0.0 copy-done.3
  115.9 10.9 %fusion.4 = f32[128,512]{1,0:T(8,128)S(1)} fusion(f32[5120,512]{1,0:T(8,128)} %all-gather.2.cloned.1.call-done, f32[5120,128]{1,0:T(8,128)S(1)} %gather_fusion, pred[5120]{0:T(1024)(128)(4,1)S(1)} %compare_and_fusion, f32[512]{0:T(512)S(1)} %copy-done.3, f32[128]{0:T(128)S(1)} %convolution_bitcast_fusion), kind=kOutput, calls=%fused_computation.5 | convolution fusion | flops 4027318272 | bytes 13377024 | tf_op jit(solution)/shard_map/dot_general | solution.py:99
  126.9 0.3 reshape_reshape.6
  127.3 3.9 %all_to_all.45 = f32[2,32,1312]{2,1,0:T(8,128)S(1)} all-to-all(f32[2,32,1312]{2,1,0:T(8,128)S(1)} %copy.28), channel_id=1, replica_groups=mesh['snap'=4,'line_0'=8,'line_1'=4,'line_2'=2] {'line_2'}, dimensions={0} | all-to-all | bytes 671744 | tf_op jit(solution)/shard_map/all_to_all | solution.py:21
  131.2 0.1 all_to_all.35
  131.3 15.7 %all_to_all.46 = f32[32,1,1312]{2,1,0:T(1,128)S(1)} all-to-all(f32[32,1,1312]{2,1,0:T(1,128)S(1)} %all_to_all.35), channel_id=1, replica_groups=mesh['snap'=4,'line_0'=8,'line_1'=4,'line_2'=2] {'line_0','line_1'}, dimensions={0} | all-to-all | bytes 335872 | tf_op jit(solution)/shard_map/all_to_all | solution.py:29
  147.0 0.1 reduce_sum.19
  147.1 0.8 broadcast_in_dim.62
  147.9 4.0 %all-to-all-start.3 = ((f32[32,1,1312]{2,1,0:T(1,128)}), f32[32,1,1312]{2,1,0:T(1,128)S(1)}, u32[]{:S(2)}, u32[]{:S(2)}) async-start(f32[32,1,1312]{2,1,0:T(1,128)} %broadcast_in_dim.62), calls=%async_computation.3 | async-start | bytes 360448 | tf_op jit(solution)/shard_map/all_to_all | solution.py:40
  151.9 0.0 copy-done.1
  151.9 0.7 constant_dynamic-slice_fusion.8
  167.6 0.0 copy-done.2
  167.6 0.7 fusion.28
  168.3 0.0 all-to-all-done.3
  168.3 5.4 %all_to_all.47 = f32[2,32,1312]{2,1,0:T(8,128)S(1)} all-to-all(f32[2,32,1312]{2,1,0:T(8,128)S(1)} %broadcast_in_dim.64), channel_id=1, replica_groups=mesh['snap'=4,'line_0'=8,'line_1'=4,'line_2'=2] {'line_2'}, dimensions={0} | all-to-all | bytes 671744 | tf_op jit(solution)/shard_map/all_to_all | solution.py:40
  173.7 0.3 copy.29
  174.0 0.4 reshape_reshape.7
  174.4 0.7 fusion.26
  177.8 0.6 fusion.27
  179.7 0.7 fusion.24
  183.1 0.7 fusion.23
  183.7 0.7 fusion.18
  185.7 1.1 multiply_subtract_fusion.5
  189.3 0.6 fusion.22
  192.5 0.7 fusion.19
  193.2 0.7 fusion.25
  200.3 0.6 fusion.21
  203.3 0.6 fusion.20
  207.8 1.0 pad_maximum_fusion.1
  208.9 1.2 fusion.7
  210.1 0.9 multiply_subtract_fusion
  (18 shorter events, 0.3 us)
Async XLA Ops:
  7.2 72.9 %copy-start = (f32[20480]{0:T(1024)S(1)}, f32[20480]{0:T(1024)}, u32[]{:S(2)}) copy-start(f32[20480]{0:T(1024)} %param.17) | copy-start | bytes 245764
  7.2 108.7 %all-gather.2.cloned.1.call-start = ((), (), s32[]{:S(2)}) async-start(), calls=%async_computation.5 | async-start | bytes 10649600 | tf_op jit(solution)/shard_map/all_gather | solution.py:101
  80.1 35.8 %copy-start.3 = (f32[512]{0:T(512)S(1)}, f32[512]{0:T(512)}, u32[]{:S(2)}) copy-start(f32[512]{0:T(512)} %param.18) | copy-start | bytes 6148
  91.0 60.9 %copy-start.1 = (s32[4,2]{0,1:T(2,128)S(1)}, s32[4,2]{0,1:T(2,128)}, u32[]{:S(2)}) copy-start(s32[4,2]{0,1:T(2,128)} %param.20) | copy-start | bytes 100
  91.0 76.6 %copy-start.2 = (f32[4]{0:T(128)S(1)}, f32[4]{0:T(128)}, u32[]{:S(2)}) copy-start(f32[4]{0:T(128)} %param.23) | copy-start | bytes 52
  147.9 20.4 %all-to-all-start.3 = ((f32[32,1,1312]{2,1,0:T(1,128)}), f32[32,1,1312]{2,1,0:T(1,128)S(1)}, u32[]{:S(2)}, u32[]{:S(2)}) async-start(f32[32,1,1312]{2,1,0:T(1,128)} %broadcast_in_dim.62), calls=%async_computation.3 | async-start | bytes 360448 | tf_op jit(solution)/shard_map/all_to_all | solution.py:40
Sparse Core Ops, SparseCore 0:
  26.8 89.0 all-gather.1
where the time goes:
time: 219 us; the launch traced here: 218 us
  between operations  72.5 us (33%)
  local copies, waits for them, and re-layouts  44.2 us (20%)
  blocking collectives  34.8 us (16%)
  waiting for transfers between devices  24.8 us (11%)
  matrix products  21.8 us (10%)
  other arithmetic  15.6 us (7%)
  starting transfers between devices  4.03 us (2%)
    all_gather x1, waiting for transfers between devices, body(): lax.all_gather(unit_blocks, LINE, axis=0, tiled=True)  24.8 us
    gather x1, local copies, waits for them, and re-layouts, body(): columns = jnp.take(ptdf_rows, order_ids, axis=1)  17.4 us
    all_to_all x1, blocking collectives, summed_rows(): lax.all_to_all(nearer, far, split_axis=0, concat_axis=0, tiled=True)  15.7 us
    unnamed x12, local copies, waits for them, and re-layouts  11.9 us
    dot_general x1, matrix products, body(): jnp.dot(columns, lax.all_gather(unit_blocks, LINE, axis=0, tiled=True), p...  10.9 us
    dot_general x1, matrix products, body(): jnp.dot(ptdf_rows, load_share, preferred_element_type=jnp.float32, precis...  10.9 us
    all_to_all x1, blocking collectives, body(): lax.all_to_all(dispatch, 'snap', split_axis=1, concat_axis=0, tiled=True)  9.81 us
    add x1, other arithmetic, body(): dispatch = held_mean + ramp_gain * (plan - lagged)  6.69 us
  transfers between devices with their start and end apart: 2, of which 1 were waited for; matrix products, arithmetic and copies ran while one was open for 22% of the time, Pallas kernels for 0%

commit v1 on v0

--- a/solution.py
+++ b/solution.py
@@ -98,7 +98,9 @@
     columns = jnp.take(ptdf_rows, order_ids, axis=1)
     gen_flows = jnp.dot(
         columns,
-        lax.all_gather(unit_blocks, LINE, axis=0, tiled=True),
+        jnp.concatenate(
+            lax.all_to_all(jnp.stack([unit_blocks] * lax.axis_size(LINE)), LINE, 0, 0), axis=0
+        ),
         preferred_element_type=jnp.float32,
         precision=lax.Precision.HIGHEST,
     )

time: 219 us -> 367 us (1.68)
  waiting for transfers between devices: 24.8 us -> 166 us
  starting transfers between devices: 4.03 us -> 18.1 us
  between operations: 72.5 us -> 58.8 us
  blocking collectives: 34.8 us -> 39.5 us
    all_to_all x0 -> x1, waiting for transfers between devices: none -> 166 us  [body(): lax.all_to_all(jnp.stack([unit_blocks] * lax.axis_size(LINE)), LINE, 0, 0)]
    all_gather x1 -> x0, waiting for transfers between devices: 24.8 us -> none  [body(): lax.all_gather(unit_blocks, LINE, axis=0, tiled=True)]
    all_to_all x0 -> x1, starting transfers between devices: none -> 14.1 us  [body(): lax.all_to_all(jnp.stack([unit_blocks] * lax.axis_size(LINE)), LINE, 0, 0)]
    another operation x0 -> x2, local copies, waits for them, and re-layouts: none -> 5.19 us  [body(): jnp.stack([unit_blocks] * lax.axis_size(LINE))]
    unnamed x12 -> x20, local copies, waits for them, and re-layouts: 11.9 us -> 11.8 us
  transfers between devices with their start and end apart: 2 -> 2, of which waited for: 1 -> 1; matrix products, arithmetic and copies ran while one was open for 22% -> 12% of each run, Pallas kernels for 0% -> 0%
where the time goes in v1:
time: 367 us; the launch traced here: 366 us
  waiting for transfers between devices  166 us (45%)
  between operations  58.8 us (16%)
  local copies, waits for them, and re-layouts  46.3 us (13%)
  blocking collectives  39.5 us (11%)
  matrix products  21.8 us (6%)
  starting transfers between devices  18.1 us (5%)
  other arithmetic  14.7 us (4%)
    all_to_all x1, waiting for transfers between devices, body(): lax.all_to_all(jnp.stack([unit_blocks] * lax.axis_size(LINE)), LINE, 0, 0)  166 us
    gather x1, local copies, waits for them, and re-layouts, body(): columns = jnp.take(ptdf_rows, order_ids, axis=1)  17.4 us
    all_to_all x1, blocking collectives, summed_rows(): lax.all_to_all(nearer, far, split_axis=0, concat_axis=0, tiled=True)  17.3 us
    all_to_all x1, starting transfers between devices, body(): lax.all_to_all(jnp.stack([unit_blocks] * lax.axis_size(LINE)), LINE, 0, 0)  14.1 us
    unnamed x20, local copies, waits for them, and re-layouts  11.8 us
    dot_general x1, matrix products, body(): jnp.dot(columns, jnp.concatenate(lax.all_to_all(jnp.stack([unit_blocks] *...  10.9 us
    dot_general x1, matrix products, body(): jnp.dot(ptdf_rows, load_share, preferred_element_type=jnp.float32, precis...  10.9 us
    all_to_all x1, blocking collectives, body(): lax.all_to_all(dispatch, 'snap', split_axis=1, concat_axis=0, tiled=True)  9.81 us
  transfers between devices with their start and end apart: 2, of which 1 were waited for; matrix products, arithmetic and copies ran while one was open for 12% of the time, Pallas kernels for 0%

profile of v1, /device:TPU:1, one launch (start us, length us, event | category | flops | bytes accessed | tf_op | source)
XLA Modules:
  0.0 365.6 jit_solution(16642601655106867987)
XLA Ops:
  0.6 0.0 copy-start
  0.6 0.7 compare_select_fusion.25
  1.4 0.7 compare_select_fusion.24
  2.0 0.7 compare_convert_fusion.23
  2.7 5.9 %multiply_add_fusion = f32[20,2048]{1,0:T(8,128)S(1)} fusion(f32[20,2048]{1,0:T(8,128)} %param.13, f32[20]{0:T(128)S(1)} %get-tuple-element.133, f32[20]{0:T(128)S(1)} %get-tuple-element.134, f32[20]{0:T(128)S(1)} %get-tuple-element.112, f32[20]{0:T(128)S(1)} %get-tuple-element.113, f32[20]{0:T(128)S(1)} %get-tuple-element.114, ...), kind=kLoop, calls=%fused_computation.11 | loop fusion | flops 3973120 | bytes 331520 | tf_op jit(solution)/shard_map/add | solution.py:95
  8.6 0.1 all_to_all.31
  8.7 0.1 copy.27
  8.8 9.8 %all_to_all.46 = f32[20,4,512]{2,0,1:T(8,128)S(1)} all-to-all(f32[20,4,512]{2,0,1:T(8,128)S(1)} %copy.27), channel_id=1, replica_groups=mesh['snap'=4,'line_0'=8,'line_1'=4,'line_2'=2] {'snap'}, dimensions={1} | all-to-all | bytes 327680 | tf_op jit(solution)/shard_map/all_to_all | solution.py:96
  18.6 5.2 %stack.19 = f32[64,80,512]{2,1,0:T(8,128)} broadcast(f32[80,512]{1,0:T(8,128)S(1)} %stack.18), dimensions={1,2} | broadcast | bytes 10649600 | tf_op jit(solution)/shard_map/stack | solution.py:102
  23.8 0.0 copy-start.1
  23.8 0.0 copy-start.6
  23.8 0.0 copy-start.4
  23.8 14.1 %all-to-all-start.1 = ((f32[64,80,512]{2,1,0:T(8,128)}), f32[64,80,512]{2,1,0:T(8,128)}, u32[]{:S(2)}, u32[]{:S(2)}) async-start(f32[64,80,512]{2,1,0:T(8,128)} %stack.19), calls=%async_computation.1 | async-start | bytes 20971520 | tf_op jit(solution)/shard_map/all_to_all | solution.py:102
  37.9 0.0 copy-done.1
  37.9 0.1 reshape.191
  38.0 0.1 copy.24
  38.1 0.2 reshape.193
  38.3 0.2 reshape.192
  38.5 0.0 copy-done.6
  38.5 0.6 fusion.31
  46.5 0.0 copy-done.3
  46.5 0.0 copy-done.4
  46.5 0.7 fusion.29
  52.2 11.8 %copy.26 = f32[128,20480]{0,1:T(8,128)} copy(f32[128,20480]{1,0:T(8,128)} %param.12) | data formatting | bytes 20971520 | tf_op args[0]
  69.0 2.0 broadcast_select_fusion.3
  71.0 0.3 maximum_bitcast_fusion
  71.4 17.4 %gather_fusion = f32[5120,128]{1,0:T(8,128)S(1)} fusion(f32[128,20480]{0,1:T(8,128)} %copy.26, s32[5120]{0:T(1024)S(1)} %broadcast_clamp_fusion), kind=kCustom, calls=%fused_computation | custom fusion | bytes 5263360 | tf_op jit(solution)/shard_map/jit(_take)/gather | solution.py:98
  88.8 0.0 copy-start.7
  88.8 0.0 copy-done
  88.8 10.9 %convolution_bitcast_fusion = f32[128]{0:T(128)S(1)} fusion(f32[128,20480]{1,0:T(8,128)} %param.12, f32[20480,1]{0,1:T(1,128)S(1)} %bitcast.65), kind=kOutput, calls=%fused_computation.6 | convolution fusion | flops 31457280 | bytes 10568192 | tf_op jit(solution)/shard_map/dot_general | solution.py:107
  99.8 0.0 copy-start.2
  99.8 0.0 copy-start.5
  99.8 166.3 %all-to-all-done.1 = f32[64,80,512]{2,1,0:T(8,128)} async-done(((f32[64,80,512]{2,1,0:T(8,128)}), f32[64,80,512]{2,1,0:T(8,128)}, u32[]{:S(2)}, u32[]{:S(2)}) %all-to-all-start.1) | async-done | bytes 10485792 | tf_op jit(solution)/shard_map/all_to_all | solution.py:102
  266.1 0.0 copy-done.7
  266.1 10.9 %fusion.4 = f32[128,512]{1,0:T(8,128)S(1)} fusion(f32[5120,512]{1,0:T(8,128)} %bitcast.3, f32[5120,128]{1,0:T(8,128)S(1)} %gather_fusion, pred[5120]{0:T(1024)(128)(4,1)S(1)} %compare_and_fusion, f32[512]{0:T(512)S(1)} %copy-done.7, f32[128]{0:T(128)S(1)} %convolution_bitcast_fusion), kind=kOutput, calls=%fused_computation.5 | convolution fusion | flops 4027318272 | bytes 13377024 | tf_op jit(solution)/shard_map/dot_general | solution.py:99
  277.1 0.3 reshape_reshape.6
  277.5 7.0 %all_to_all.47 = f32[2,32,1312]{2,1,0:T(8,128)S(1)} all-to-all(f32[2,32,1312]{2,1,0:T(8,128)S(1)} %copy.28), channel_id=1, replica_groups=mesh['snap'=4,'line_0'=8,'line_1'=4,'line_2'=2] {'line_2'}, dimensions={0} | all-to-all | bytes 671744 | tf_op jit(solution)/shard_map/all_to_all | solution.py:21
  284.6 0.1 all_to_all.36
  284.7 17.3 %all_to_all.48 = f32[32,1,1312]{2,1,0:T(1,128)S(1)} all-to-all(f32[32,1,1312]{2,1,0:T(1,128)S(1)} %all_to_all.36), channel_id=1, replica_groups=mesh['snap'=4,'line_0'=8,'line_1'=4,'line_2'=2] {'line_0','line_1'}, dimensions={0} | all-to-all | bytes 335872 | tf_op jit(solution)/shard_map/all_to_all | solution.py:29
  302.0 0.1 reduce_sum.19
  302.1 0.8 broadcast_in_dim.62
  302.9 4.0 %all-to-all-start.4 = ((f32[32,1,1312]{2,1,0:T(1,128)}), f32[32,1,1312]{2,1,0:T(1,128)S(1)}, u32[]{:S(2)}, u32[]{:S(2)}) async-start(f32[32,1,1312]{2,1,0:T(1,128)} %broadcast_in_dim.62), calls=%async_computation.4 | async-start | bytes 360448 | tf_op jit(solution)/shard_map/all_to_all | solution.py:40
  306.9 0.0 copy-done.2
  306.9 0.7 constant_dynamic-slice_fusion.8
  322.5 0.0 copy-done.5
  322.5 0.6 fusion.28
  323.1 0.0 all-to-all-done.4
  323.2 5.4 %all_to_all.49 = f32[2,32,1312]{2,1,0:T(8,128)S(1)} all-to-all(f32[2,32,1312]{2,1,0:T(8,128)S(1)} %broadcast_in_dim.64), channel_id=1, replica_groups=mesh['snap'=4,'line_0'=8,'line_1'=4,'line_2'=2] {'line_2'}, dimensions={0} | all-to-all | bytes 671744 | tf_op jit(solution)/shard_map/all_to_all | solution.py:40
  328.6 0.3 copy.29
  328.9 0.4 reshape_reshape.7
  329.3 0.6 fusion.26
  332.5 0.6 fusion.27
  334.4 0.6 fusion.24
  337.6 0.7 fusion.23
  338.3 0.7 fusion.18
  340.3 1.1 multiply_subtract_fusion.5
  344.0 0.7 fusion.22
  347.3 0.7 fusion.19
  348.0 0.7 fusion.25
  354.9 0.7 fusion.21
  358.1 0.6 fusion.20
  362.5 1.0 pad_maximum_fusion.1
  363.6 1.2 fusion.7
  364.7 0.9 multiply_subtract_fusion
  (20 shorter events, 0.4 us)
Async XLA Ops:
  0.6 88.2 %copy-start = (f32[20480]{0:T(1024)S(1)}, f32[20480]{0:T(1024)}, u32[]{:S(2)}) copy-start(f32[20480]{0:T(1024)} %param.17) | copy-start | bytes 245764
  23.8 14.1 %copy-start.1 = (s32[5120]{0:T(1024)S(1)}, s32[5120]{0:T(1024)}, u32[]{:S(2)}) copy-start(s32[5120]{0:T(1024)} %param.14) | copy-start | bytes 61444
  23.8 14.7 %copy-start.6 = (s32[4]{0:T(128)S(1)}, s32[4]{0:T(128)}, u32[]{:S(2)}) copy-start(s32[4]{0:T(128)} %param.19) | copy-start | bytes 52
  23.8 22.7 %copy-start.3 = (s32[4]{0:T(128)S(1)}, s32[4]{0:T(128)}, u32[]{:S(2)}) copy-start(s32[4]{0:T(128)} %param.22) | copy-start | bytes 52
  23.8 22.7 %copy-start.4 = (s32[4]{0:T(128)S(1)}, s32[4]{0:T(128)}, u32[]{:S(2)}) copy-start(s32[4]{0:T(128)} %param.21) | copy-start | bytes 52
  23.8 242.3 %all-to-all-start.1 = ((f32[64,80,512]{2,1,0:T(8,128)}), f32[64,80,512]{2,1,0:T(8,128)}, u32[]{:S(2)}, u32[]{:S(2)}) async-start(f32[64,80,512]{2,1,0:T(8,128)} %stack.19), calls=%async_computation.1 | async-start | bytes 20971520 | tf_op jit(solution)/shard_map/all_to_all | solution.py:102
  88.8 177.3 %copy-start.7 = (f32[512]{0:T(512)S(1)}, f32[512]{0:T(512)}, u32[]{:S(2)}) copy-start(f32[512]{0:T(512)} %param.18) | copy-start | bytes 6148
  99.8 207.1 %copy-start.2 = (s32[4,2]{0,1:T(2,128)S(1)}, s32[4,2]{0,1:T(2,128)}, u32[]{:S(2)}) copy-start(s32[4,2]{0,1:T(2,128)} %param.20) | copy-start | bytes 100
  99.8 222.7 %copy-start.5 = (f32[4]{0:T(128)S(1)}, f32[4]{0:T(128)}, u32[]{:S(2)}) copy-start(f32[4]{0:T(128)} %param.23) | copy-start | bytes 52
  302.9 20.2 %all-to-all-start.4 = ((f32[32,1,1312]{2,1,0:T(1,128)}), f32[32,1,1312]{2,1,0:T(1,128)S(1)}, u32[]{:S(2)}, u32[]{:S(2)}) async-start(f32[32,1,1312]{2,1,0:T(1,128)} %broadcast_in_dim.62), calls=%async_computation.4 | async-start | bytes 360448 | tf_op jit(solution)/shard_map/all_to_all | solution.py:40
